TPU v7x, 32 devices: a whole 2x2x4 slice. The times are simulated.
32 devices in a mesh: tok: 2 (over x), voc: 4 (over y, core), wid: 4 (over z).
Axes of the slice: x: 2, y: 2, z: 4, core: 2. Of those that a mesh axis runs over, the one named last changes fastest.
Arguments:
- hidden: bfloat16 [512, 8192], P('tok', 'wid'), may hold values from -1500 to 1500
- proj: bfloat16 [3584, 8192], P('voc', 'wid'), may hold values from -0.0625 to 0.0625
- table: bfloat16 [19456, 3584], P(('voc', 'wid'), 'tok'), may hold values from -10 to 10
- targets: int32 [512], P('tok'), may hold values from 0 to 19455
- valid: int32 [512], P('tok'), may hold values from 0 to 1, as said below
Outputs:
- grad_proj: float32 [3584, 8192], P('voc', 'wid')
- loss: float32 [], replicated
Inputs may be any that keep to these rules, and one draw needn't show every extreme that they name: `valid`: position 0 is always scored.
All inputs are finite; a program needn't handle non-finite values.
Results may differ from a plain program's by a relative error of at most 0.008.
Values may be sent and summed in bfloat16 or wider, within the bound.
No kernel may reach another device: no remote copies, remote signals or barrier semaphores. Data moves between devices by JAX's collectives and lax.ppermute only.
A program may use at most 128 MiB of HBM per device.

v0:
```python
import jax
import jax.numpy as jnp
from jax import lax
from jax.sharding import PartitionSpec as P


def on_device(hidden, proj, table, targets, valid):
    tok_rows = hidden.shape[0]
    block_rows = table.shape[0]
    partial_value = lax.dot_general(
        hidden, proj, (((1,), (1,)), ((), ())), preferred_element_type=jnp.float32
    )
    summed = lax.psum(partial_value, "wid")
    projected = lax.all_gather(summed.astype(jnp.bfloat16), "voc", axis=1, tiled=True)
    full_table = lax.all_gather(table, "tok", axis=1, tiled=True)
    logits = lax.dot_general(
        projected, full_table, (((1,), (1,)), ((), ())), preferred_element_type=jnp.float32
    )
    block_base = (lax.axis_index("voc") * lax.axis_size("wid") + lax.axis_index("wid")) * block_rows
    local_ids = targets - block_base
    is_target = local_ids[:, None] == lax.broadcasted_iota(jnp.int32, (tok_rows, block_rows), 1)
    picked_here = jnp.sum(jnp.where(is_target, logits, 0.0), axis=1)
    peak_here = jnp.max(logits, axis=1)
    row_peak = lax.pmax(peak_here, ("voc", "wid"))
    exp_here = jnp.sum(jnp.exp(logits - row_peak[:, None]), axis=1)
    row_total, picked = lax.psum((exp_here, picked_here), ("voc", "wid"))
    log_total = row_peak + jnp.log(row_total)
    weight = valid.astype(jnp.float32)
    dlogits = (
        weight[:, None] * (jnp.exp(logits - log_total[:, None]) - is_target.astype(jnp.float32))
    ).astype(jnp.bfloat16)
    reduced = lax.psum_scatter(
        lax.dot_general(
            full_table, dlogits, (((0,), (1,)), ((), ())), preferred_element_type=jnp.float32
        ),
        "voc",
        scatter_dimension=0,
        tiled=True,
    )
    grad_rows = lax.psum(reduced, "wid").astype(jnp.bfloat16)
    grad_part = jnp.dot(grad_rows, hidden, preferred_element_type=jnp.float32)
    loss_part = jnp.sum(weight * (log_total - picked))
    count_part = jnp.sum(weight)
    grad_proj, loss_sum, position_count = lax.psum((grad_part, loss_part, count_part), "tok")
    return (grad_proj, loss_sum / position_count)


def solution(mesh):
    return jax.shard_map(
        on_device,
        mesh=mesh,
        in_specs=(P("tok", "wid"), P("voc", "wid"), P(("voc", "wid"), "tok"), P("tok"), P("tok")),
        out_specs=(P("voc", "wid"), P()),
        check_vma=False,
    )
```

profile of v0, /device:TPU:0, one launch (start us, length us, event | category | flops | bytes accessed | tf_op | source)
XLA Modules:
  0.0 535.9 jit_solution(15466897181801371139)
XLA Ops:
  7.2 0.0 copy-start
  7.2 0.0 all-gather.3.cloned.1.call-start
  7.2 1.2 copy-done
  8.4 3.3 fusion.6
  11.7 41.0 %all-reduce.7 = bf16[256,896]{1,0:T(8,128)(2,1)} all-reduce(f32[256,896]{1,0:T(8,128)S(1)} %fusion.6), channel_id=1, replica_groups=mesh['tok'=2,'voc'=4,'wid'=4] {'wid'}, use_global_device_ids=true, to_apply=%region_0.0 | all-reduce | flops 229376 | bytes 1376256 | tf_op jit(solution)/shard_map/psum | solution.py:13
  52.7 0.0 all-gather.3.cloned.1.call-update
  52.7 0.0 copy-start.1
  52.7 0.0 copy-start.2
  52.7 0.0 all-gather.5.cloned.1.call-start
  52.8 0.7 all-gather.5.cloned.1.call-update
  53.5 0.0 reduce-scatter.2.cloned.1.call-start
  53.5 0.0 copy-done.1
  53.6 0.0 copy-done.2
  53.6 19.9 %all-gather.3.cloned.1.call-done = bf16[256,3584]{1,0:T(8,128)(2,1)} async-done(((bf16[256,896]{1,0:T(8,128)(2,1)}), bf16[256,3584]{1,0:T(8,128)(2,1)}) %all-gather.3.cloned.1.call-update) | async-done | bytes 1835024 | tf_op jit(solution)/shard_map/all_gather | solution.py:14
  73.5 111.7 %all-gather.5.cloned.1.call-done = bf16[1216,3584]{1,0:T(8,128)(2,1)} async-done(((bf16[1216,1792]{1,0:T(8,128)(2,1)}), bf16[1216,3584]{1,0:T(8,128)(2,1)}) %all-gather.5.cloned.1.call-update) | async-done | bytes 8716304 | tf_op jit(solution)/shard_map/all_gather | solution.py:15
  185.1 6.5 %fusion.5 = (f32[256]{0:T(256)S(1)}, f32[256,1216]{0,1:T(8,128)S(1)}) fusion(bf16[256,3584]{1,0:T(8,128)(2,1)} %all-gather.3.cloned.1.call-done, bf16[1216,3584]{1,0:T(8,128)(2,1)} %all-gather.5.cloned.1.call-done), kind=kOutput, calls=%fused_computation.14 | convolution fusion | flops 2231680768 | bytes 11797504 | tf_op jit(solution)/shard_map/dot_general | solution.py:16
  191.6 33.4 %pmax.7 = f32[256]{0:T(256)S(1)} all-reduce(f32[256]{0:T(256)S(1)} %get-tuple-element.11), channel_id=1, replica_groups=mesh['tok'=2,'voc'=4,'wid'=4] {'voc','wid'}, use_global_device_ids=true, to_apply=%region_2.3 | all-reduce | flops 256 | bytes 2048 | tf_op jit(solution)/shard_map/pmax | solution.py:24
  225.0 0.3 select_reduce_fusion
  225.4 29.7 %all-reduce = (f32[256]{0:T(256)S(1)}, f32[256]{0:T(256)S(1)}) all-reduce(f32[256]{0:T(256)S(1)} %get-tuple-element.3, f32[256]{0:T(256)S(1)} %get-tuple-element.2), channel_id=1, replica_groups=mesh['tok'=2,'voc'=4,'wid'=4] {'voc','wid'}, use_global_device_ids=true, to_apply=%region_4.5 | all-reduce | flops 512 | bytes 4096 | tf_op jit(solution)/shard_map/psum | solution.py:26
  255.0 0.6 convert_reduce_fusion
  255.7 7.9 %convolution_bitcast_fusion = f32[3584,256]{0,1:T(8,128)} fusion(bf16[1216,3584]{1,0:T(8,128)(2,1)} %all-gather.5.cloned.1.call-done, f32[256,1216]{0,1:T(8,128)S(1)} %get-tuple-element.12, s32[256]{0:T(256)S(1)} %broadcast_subtract_fusion, f32[256]{0:T(256)S(1)} %get-tuple-element.10, f32[256]{0:T(256)S(1)} %convert_element_type.15), kind=kOutput, calls=%fused_computation | convolution fusion | flops 2233237504 | bytes 13634560 | tf_op jit(solution)/shard_map/dot_general | solution.py:33
  263.6 0.0 reduce-scatter.2.cloned.1.call-update
  263.6 0.0 all-reduce.6.cloned.1.call-start
  263.7 39.4 %reduce-scatter.2.cloned.1.call-done = f32[896,256]{0,1:T(8,128)} async-done(((f32[3584,256]{0,1:T(8,128)}), f32[896,256]{0,1:T(8,128)}) %reduce-scatter.2.cloned.1.call-update) | async-done | bytes 917520 | tf_op jit(solution)/shard_map/reduce_scatter | solution.py:32
  303.1 39.8 %all-reduce.8 = bf16[896,256]{0,1:T(8,128)(2,1)S(1)} all-reduce(f32[896,256]{0,1:T(8,128)} %reduce-scatter.2.cloned.1.call-done), channel_id=1, replica_groups=mesh['tok'=2,'voc'=4,'wid'=4] {'wid'}, use_global_device_ids=true, to_apply=%region_6.7 | all-reduce | flops 229376 | bytes 1376256 | tf_op jit(solution)/shard_map/psum | solution.py:40
  342.9 4.2 fusion.7
  347.1 0.0 all-reduce.6.cloned.1.call-update
  347.1 5.7 %all-reduce.1 = (f32[]{:T(128)}, f32[]{:T(128)}) all-reduce(f32[]{:T(128)} %get-tuple-element.5, f32[]{:T(128)} %get-tuple-element.4), channel_id=1, replica_groups=mesh['tok'=2,'voc'=4,'wid'=4] {'tok'}, use_global_device_ids=true, to_apply=%region_11.12 | all-reduce | flops 2 | bytes 16 | tf_op jit(solution)/shard_map/psum | solution.py:44
  354.2 167.0 %all-reduce.6.cloned.1.call-done = f32[896,2048]{1,0:T(8,128)} async-done(((f32[896,2048]{1,0:T(8,128)}), f32[896,2048]{1,0:T(8,128)}) %all-reduce.6.cloned.1.call-update) | async-done | bytes 7340048 | tf_op jit(solution)/shard_map/psum | solution.py:44
  521.2 7.1 %copy.12 = f32[896,2048]{1,0:T(8,128)} copy(f32[896,2048]{1,0:T(8,128)} %all-reduce.6.cloned.1.call-done) | data formatting | bytes 14680064
  (2 shorter events, 0.0 us)
Async XLA Ops:
  7.2 1.2 copy-start
  7.2 66.3 %all-gather.3.cloned.1.call-start = ((), (), s32[]{:S(2)}) async-start(), calls=%async_computation.1 | async-start | bytes 2293760 | tf_op jit(solution)/shard_map/all_gather | solution.py:14
  52.7 0.8 copy-start.1
  52.7 0.8 copy-start.2
  52.7 132.4 %all-gather.5.cloned.1.call-start = ((), (), s32[]{:S(2)}) async-start(), calls=%async_computation.2 | async-start | bytes 13074432 | tf_op jit(solution)/shard_map/all_gather | solution.py:15
  53.5 249.6 %reduce-scatter.2.cloned.1.call-start = ((), (), s32[]{:S(2)}) async-start(), calls=%async_computation.3 | async-start | bytes 4587520 | tf_op jit(solution)/shard_map/reduce_scatter | solution.py:32
  263.6 257.6 %all-reduce.6.cloned.1.call-start = ((), (), s32[]{:S(2)}) async-start(), calls=%async_computation.4 | async-start | bytes 14680064 | tf_op jit(solution)/shard_map/psum | solution.py:44
Sparse Core Ops, SparseCore 0:
  52.8 20.5 all-gather.2
  75.0 110.0 all-gather.4
  263.7 39.2 reduce-scatter.1
  347.3 173.8 all-reduce.5
where the time goes:
time: 536 us
  waiting for transfers between devices  339 us (63%)
  blocking collectives  150 us (28%)
  matrix products  21.9 us (4%)
  between operations  16.4 us (3%)
  local copies, waits for them, and re-layouts  8.27 us (2%)
    psum x1, waiting for transfers between devices, on_device(): lax.psum((grad_part, loss_part, count_part), 'tok')  167 us
    all_gather x1, waiting for transfers between devices, on_device(): full_table = lax.all_gather(table, 'tok', axis=1, tiled=True)  112 us
    psum x1, blocking collectives, on_device(): summed = lax.psum(partial_value, 'wid')  41 us
    psum x1, blocking collectives, on_device(): grad_rows = lax.psum(reduced, 'wid').astype(jnp.bfloat16)  39.8 us
    reduce_scatter x1, waiting for transfers between devices, on_device(): lax.psum_scatter(lax.dot_general(full_table, dlogits, (((0,), (1,)), ((),...  39.4 us
    pmax x1, blocking collectives, on_device(): row_peak = lax.pmax(peak_here, ('voc', 'wid'))  33.4 us
    psum x1, blocking collectives, on_device(): row_total, picked = lax.psum((exp_here, picked_here), ('voc', 'wid'))  29.7 us
    all_gather x1, waiting for transfers between devices, on_device(): lax.all_gather(summed.astype(jnp.bfloat16), 'voc', axis=1, tiled=True)  19.9 us
  transfers between devices with their start and end apart: 4, of which 4 were waited for; matrix products, arithmetic and copies ran while one was open for 0% of the time, Pallas kernels for 0%

commit v1 on v0

--- a/solution.py
+++ b/solution.py
@@ -10,7 +10,8 @@
     partial_value = lax.dot_general(
         hidden, proj, (((1,), (1,)), ((), ())), preferred_element_type=jnp.float32
     )
-    summed = lax.psum(partial_value, "wid")
+    shards = lax.all_gather(partial_value, "wid", axis=0, tiled=False)
+    summed = shards.sum(axis=0)
     projected = lax.all_gather(summed.astype(jnp.bfloat16), "voc", axis=1, tiled=True)
     full_table = lax.all_gather(table, "tok", axis=1, tiled=True)
     logits = lax.dot_general(

time: 536 us -> 574 us (1.071)
  waiting for transfers between devices: 339 us -> 413 us
  blocking collectives: 150 us -> 109 us
    all_gather x0 -> x1, waiting for transfers between devices: none -> 74.9 us  [on_device(): shards = lax.all_gather(partial_value, 'wid', axis=0, tiled=False)]
    psum x1 -> x0, blocking collectives: 41 us -> none  [on_device(): summed = lax.psum(partial_value, 'wid')]
  transfers between devices with their start and end apart: 4 -> 5, of which waited for: 4 -> 5; matrix products, arithmetic and copies ran while one was open for 0% -> 0% of each run, Pallas kernels for 0% -> 0%
where the time goes in v1:
time: 574 us; the launch traced here: 573 us
  waiting for transfers between devices  413 us (72%)
  blocking collectives  109 us (19%)
  matrix products  22.9 us (4%)
  between operations  16.4 us (3%)
  local copies, waits for them, and re-layouts  8.27 us (1%)
    psum x1, waiting for transfers between devices, on_device(): lax.psum((grad_part, loss_part, count_part), 'tok')  167 us
    all_gather x1, waiting for transfers between devices, on_device(): full_table = lax.all_gather(table, 'tok', axis=1, tiled=True)  112 us
    all_gather x1, waiting for transfers between devices, on_device(): shards = lax.all_gather(partial_value, 'wid', axis=0, tiled=False)  74.9 us
    psum x1, blocking collectives, on_device(): grad_rows = lax.psum(reduced, 'wid').astype(jnp.bfloat16)  39.9 us
    reduce_scatter x1, waiting for transfers between devices, on_device(): lax.psum_scatter(lax.dot_general(full_table, dlogits, (((0,), (1,)), ((),...  39.4 us
    pmax x1, blocking collectives, on_device(): row_peak = lax.pmax(peak_here, ('voc', 'wid'))  33.4 us
    psum x1, blocking collectives, on_device(): row_total, picked = lax.psum((exp_here, picked_here), ('voc', 'wid'))  29.7 us
    all_gather x1, waiting for transfers between devices, on_device(): lax.all_gather(summed.astype(jnp.bfloat16), 'voc', axis=1, tiled=True)  19 us
  transfers between devices with their start and end apart: 5, of which 5 were waited for; matrix products, arithmetic and copies ran while one was open for 0% of the time, Pallas kernels for 0%

profile of v1, /device:TPU:0, one launch (start us, length us, event | category | flops | bytes accessed | tf_op | source)
XLA Modules:
  0.0 573.2 jit_solution(4906249613210148052)
XLA Ops:
  7.2 0.0 copy-start
  7.2 0.0 all-gather.9.cloned.1.call-start
  7.2 1.2 copy-done
  8.4 4.2 fusion.6
  12.6 0.0 all-gather.9.cloned.1.call-update
  12.7 0.0 all-gather.5.cloned.1.call-start
  12.7 74.9 %all-gather.9.cloned.1.call-done = f32[1024,896]{1,0:T(8,128)} async-done(((f32[256,896]{1,0:T(8,128)}), f32[1024,896]{1,0:T(8,128)}) %all-gather.9.cloned.1.call-update) | async-done | bytes 3670032 | tf_op jit(solution)/shard_map/all_gather | solution.py:13
  87.6 3.1 reduce_sum.45
  90.8 0.0 all-gather.5.cloned.1.call-update
  90.8 0.0 copy-start.1
  90.8 0.0 copy-start.2
  90.8 0.0 all-gather.7.cloned.1.call-start
  90.9 0.7 all-gather.7.cloned.1.call-update
  91.6 0.0 reduce-scatter.2.cloned.1.call-start
  91.6 0.0 copy-done.1
  91.6 0.0 copy-done.2
  91.7 19.0 %all-gather.5.cloned.1.call-done = bf16[256,3584]{1,0:T(8,128)(2,1)} async-done(((bf16[256,896]{1,0:T(8,128)(2,1)}), bf16[256,3584]{1,0:T(8,128)(2,1)}) %all-gather.5.cloned.1.call-update) | async-done | bytes 1835024 | tf_op jit(solution)/shard_map/all_gather | solution.py:15
  110.7 111.7 %all-gather.7.cloned.1.call-done = bf16[1216,3584]{1,0:T(8,128)(2,1)} async-done(((bf16[1216,1792]{1,0:T(8,128)(2,1)}), bf16[1216,3584]{1,0:T(8,128)(2,1)}) %all-gather.7.cloned.1.call-update) | async-done | bytes 8716304 | tf_op jit(solution)/shard_map/all_gather | solution.py:16
  222.4 6.5 %fusion.5 = (f32[256]{0:T(256)S(1)}, f32[256,1216]{0,1:T(8,128)S(1)}) fusion(bf16[256,3584]{1,0:T(8,128)(2,1)} %all-gather.5.cloned.1.call-done, bf16[1216,3584]{1,0:T(8,128)(2,1)} %all-gather.7.cloned.1.call-done), kind=kOutput, calls=%fused_computation.14 | convolution fusion | flops 2231680768 | bytes 11797504 | tf_op jit(solution)/shard_map/dot_general | solution.py:17
  228.9 33.4 %pmax.7 = f32[256]{0:T(256)S(1)} all-reduce(f32[256]{0:T(256)S(1)} %get-tuple-element.11), channel_id=1, replica_groups=mesh['tok'=2,'voc'=4,'wid'=4] {'voc','wid'}, use_global_device_ids=true, to_apply=%region_2.3 | all-reduce | flops 256 | bytes 2048 | tf_op jit(solution)/shard_map/pmax | solution.py:25
  262.3 0.3 select_reduce_fusion
  262.6 29.7 %all-reduce = (f32[256]{0:T(256)S(1)}, f32[256]{0:T(256)S(1)}) all-reduce(f32[256]{0:T(256)S(1)} %get-tuple-element.3, f32[256]{0:T(256)S(1)} %get-tuple-element.2), channel_id=1, replica_groups=mesh['tok'=2,'voc'=4,'wid'=4] {'voc','wid'}, use_global_device_ids=true, to_apply=%region_4.5 | all-reduce | flops 512 | bytes 4096 | tf_op jit(solution)/shard_map/psum | solution.py:27
  292.3 0.6 convert_reduce_fusion
  292.9 7.9 %convolution_bitcast_fusion = f32[3584,256]{0,1:T(8,128)} fusion(bf16[1216,3584]{1,0:T(8,128)(2,1)} %all-gather.7.cloned.1.call-done, f32[256,1216]{0,1:T(8,128)S(1)} %get-tuple-element.12, s32[256]{0:T(256)S(1)} %broadcast_subtract_fusion, f32[256]{0:T(256)S(1)} %get-tuple-element.10, f32[256]{0:T(256)S(1)} %convert_element_type.15), kind=kOutput, calls=%fused_computation | convolution fusion | flops 2233237504 | bytes 13634560 | tf_op jit(solution)/shard_map/dot_general | solution.py:34
  300.8 0.0 reduce-scatter.2.cloned.1.call-update
  300.9 0.0 all-reduce.5.cloned.1.call-start
  300.9 39.4 %reduce-scatter.2.cloned.1.call-done = f32[896,256]{0,1:T(8,128)} async-done(((f32[3584,256]{0,1:T(8,128)}), f32[896,256]{0,1:T(8,128)}) %reduce-scatter.2.cloned.1.call-update) | async-done | bytes 917520 | tf_op jit(solution)/shard_map/reduce_scatter | solution.py:33
  340.3 39.9 %all-reduce.6 = bf16[896,256]{0,1:T(8,128)(2,1)S(1)} all-reduce(f32[896,256]{0,1:T(8,128)} %reduce-scatter.2.cloned.1.call-done), channel_id=1, replica_groups=mesh['tok'=2,'voc'=4,'wid'=4] {'wid'}, use_global_device_ids=true, to_apply=%region_6.7 | all-reduce | flops 229376 | bytes 1376256 | tf_op jit(solution)/shard_map/psum | solution.py:41
  380.2 4.2 fusion.7
  384.4 0.0 all-reduce.5.cloned.1.call-update
  384.4 5.7 all-reduce.1
  391.4 167.0 %all-reduce.5.cloned.1.call-done = f32[896,2048]{1,0:T(8,128)} async-done(((f32[896,2048]{1,0:T(8,128)}), f32[896,2048]{1,0:T(8,128)}) %all-reduce.5.cloned.1.call-update) | async-done | bytes 7340048 | tf_op jit(solution)/shard_map/psum | solution.py:45
  558.4 7.1 %copy.10 = f32[896,2048]{1,0:T(8,128)} copy(f32[896,2048]{1,0:T(8,128)} %all-reduce.5.cloned.1.call-done) | data formatting | bytes 14680064
  (2 shorter events, 0.0 us)
Async XLA Ops:
  7.2 1.2 copy-start
  7.2 80.4 %all-gather.9.cloned.1.call-start = ((), (), s32[]{:S(2)}) async-start(), calls=%async_computation.5 | async-start | bytes 4587520 | tf_op jit(solution)/shard_map/all_gather | solution.py:13
  12.7 98.0 %all-gather.5.cloned.1.call-start = ((), (), s32[]{:S(2)}) async-start(), calls=%async_computation.1 | async-start | bytes 2293760 | tf_op jit(solution)/shard_map/all_gather | solution.py:15
  90.8 0.8 copy-start.1
  90.8 0.8 copy-start.2
  90.8 131.5 %all-gather.7.cloned.1.call-start = ((), (), s32[]{:S(2)}) async-start(), calls=%async_computation.2 | async-start | bytes 13074432 | tf_op jit(solution)/shard_map/all_gather | solution.py:16
  91.6 248.7 %reduce-scatter.2.cloned.1.call-start = ((), (), s32[]{:S(2)}) async-start(), calls=%async_computation.3 | async-start | bytes 4587520 | tf_op jit(solution)/shard_map/reduce_scatter | solution.py:33
  300.9 257.6 %all-reduce.5.cloned.1.call-start = ((), (), s32[]{:S(2)}) async-start(), calls=%async_computation.4 | async-start | bytes 14680064 | tf_op jit(solution)/shard_map/psum | solution.py:45
Sparse Core Ops, SparseCore 0:
  12.8 74.7 all-gather.8
  90.9 19.7 all-gather.4
  112.2 110.0 all-gather.6
  301.0 39.2 reduce-scatter.1
  384.5 173.8 all-reduce.4
